TPU v7x, 256 devices: a whole 4x4x8 slice. The times are simulated.
256 devices in a mesh: gx: 8 (over x, core), gy: 32 (over y, z).
Axes of the slice: x: 4, y: 4, z: 8, core: 2. Of those that a mesh axis runs over, the one named last changes fastest.
Arguments:
- hidden_in: bfloat16 [8192, 4096], P('gx', 'gy')
- norm_gain: bfloat16 [4096], P('gy'), may hold values from 0.099609375 to 1.8984375
- query_proj: bfloat16 [4096, 4096], P('gx', 'gy')
- kv_proj: bfloat16 [1024, 4096], P(None, 'gy')
- prompt_lengths: int32 [8], replicated, may hold values from 1 to 4096, 8192 in all
- cache_slot: int32 [512], replicated, may hold values from 0 to 511, as said below
Outputs:
- attention: bfloat16 [8192, 4096], P('gy', 'gx')
- kv_cache: bfloat16 [512, 16, 1024], P('gy', None, 'gx')
Inputs may be any that keep to these rules, and one draw needn't show every extreme that they name: `prompt_lengths`: the 8 prompts sum to 8192 tokens; the longest has exactly 4096. `cache_slot`: A permutation of the 512 slots; slot s is held by index s // 16 of gy. The 16 pages of one token block go to any one index at most 1 times, and every index receives exactly 16 pages.
All inputs are finite; a program needn't handle non-finite values.
Results may differ from a plain program's by a relative error of at most 0.0066.
The roundings to bfloat16 on the way count: a program that leaves them out, or rounds other values in their place, can miss the bound.
Values may be sent and summed in bfloat16 or wider, within the bound.
No kernel may reach another device: no remote copies, remote signals or barrier semaphores. Data moves between devices by JAX's collectives and lax.ppermute only.
A program may use at most 128 MiB of HBM per device.

v0:
```python
import math
import jax
import jax.numpy as jnp
from jax import lax
from jax.sharding import PartitionSpec as P

D = 4096
H = 32
KVH = 4
HD = 128
PAGES_DEV = 16
MOST = 4096
epsilon = 1e-06
rope_base = 5000000.0
masked_out = -1e30


def token_places(prompt_lengths, token_index):
    prompt_ends = jnp.cumsum(prompt_lengths)
    prompt_starts = prompt_ends - prompt_lengths
    segment = jnp.sum((token_index[:, None] >= prompt_ends[None, :]).astype(jnp.int32), axis=1)
    chosen = segment[:, None] == jnp.arange(prompt_lengths.shape[0], dtype=jnp.int32)[None, :]
    opening = jnp.sum(jnp.where(chosen, prompt_starts[None, :], 0), axis=1)
    return (segment, token_index - opening)


def rotate(vectors, places):
    half_size = vectors.shape[-1] // 2
    frequency = rope_base ** (-(jnp.arange(half_size, dtype=jnp.float32) * 2.0) / vectors.shape[-1])
    angles = places.astype(jnp.float32)[:, None] * frequency[None, :]
    cos_part = jnp.cos(angles)[:, None, :]
    sin_part = jnp.sin(angles)[:, None, :]
    leading = vectors[..., :half_size]
    trailing = vectors[..., half_size:]
    return jnp.concatenate(
        [leading * cos_part - trailing * sin_part, trailing * cos_part + leading * sin_part],
        axis=-1,
    )


def local(hidden_in, norm_gain, query_proj, kv_proj, prompt_lengths, cache_slot):
    count_gx = lax.axis_size("gx")
    count_gy = lax.axis_size("gy")
    where_gx = lax.axis_index("gx")
    where_gy = lax.axis_index("gy")
    local_rows, local_feats = hidden_in.shape
    features = local_feats * count_gy
    block_tokens = local_rows * count_gx // count_gy
    all_tokens = block_tokens * count_gy
    blocks_per_slab = local_rows // block_tokens
    sub = block_tokens // count_gy
    heads_here = query_proj.shape[0] // HD
    query_cols = heads_here * HD
    is_key = where_gx % 2 == 0
    kv_rows = lax.dynamic_slice_in_dim(kv_proj, where_gx * HD, HD, 0)
    gain_rows = jnp.concatenate(
        [norm_gain[None, :], jnp.zeros((7, local_feats), norm_gain.dtype)], axis=0
    )
    stacked = jnp.concatenate([query_proj, kv_rows, gain_rows], axis=0)
    gathered = lax.all_gather(stacked, "gy", axis=1, tiled=True)
    weight_rows = query_cols + HD
    weights_full = gathered[:weight_rows]
    gain_full = gathered[weight_rows]
    pieces = hidden_in.reshape(blocks_per_slab, count_gy, sub, local_feats)
    pieces = lax.all_to_all(pieces, "gy", 1, 1, tiled=True)
    spread = jnp.broadcast_to(pieces[None], (count_gx,) + pieces.shape)
    rows_here = lax.all_to_all(spread, "gx", 0, 0, tiled=True)
    rows_here = rows_here.transpose(0, 1, 3, 2, 4).reshape(block_tokens, features)
    widened = rows_here.astype(jnp.float32)
    squares = jnp.sum(widened * widened, axis=1)
    normed = (
        widened
        * lax.rsqrt(squares / features + epsilon)[:, None]
        * gain_full.astype(jnp.float32)[None, :]
    ).astype(jnp.bfloat16)
    contract = (((1,), (1,)), ((), ()))
    projected = lax.dot_general(normed, weights_full, contract, preferred_element_type=jnp.float32)
    order = jnp.arange(block_tokens, dtype=jnp.int32)
    my_tokens = order // sub * block_tokens + where_gy * sub + order % sub
    unused_segment, my_places = token_places(prompt_lengths, my_tokens)
    queries = rotate(
        projected[:, :query_cols].reshape(block_tokens, heads_here, HD), my_places
    ).astype(jnp.bfloat16)
    half_raw = projected[:, query_cols:]
    rotated = rotate(half_raw[:, None, :], my_places)[:, 0, :]
    mine = jnp.where(is_key, rotated, half_raw).astype(jnp.bfloat16)
    window_blocks = min(count_gy, MOST // block_tokens + 1)
    window = window_blocks * block_tokens
    first_blocks = [
        min(max(b - (window_blocks - 1), 0), count_gy - window_blocks) for b in range(count_gy)
    ]
    chosen = jnp.asarray(
        [[f + w for w in range(window_blocks)] for f in first_blocks], dtype=jnp.int32
    )
    strided = mine.reshape(count_gy, sub, HD)
    kv_parcel = jnp.take(strided, chosen, axis=0).reshape(count_gy, window_blocks * sub * HD)
    q_parcel = queries.reshape(count_gy, sub * query_cols)
    parcel = jnp.concatenate([q_parcel, kv_parcel], axis=1)
    arrived = lax.all_to_all(parcel, "gy", 0, 0, tiled=True)
    queries = arrived[:, : sub * query_cols].reshape(block_tokens, heads_here, HD)
    mine_window = arrived[:, sub * query_cols :].reshape(count_gy, window_blocks, sub, HD)
    other_window = lax.ppermute(mine_window, "gx", [(p, p ^ 1) for p in range(count_gx)])
    key_rows = jnp.where(is_key, mine_window, other_window).reshape(window, HD)
    value_rows = jnp.where(is_key, other_window, mine_window).reshape(window, HD)
    first_query = where_gy * block_tokens
    token_index = first_query + order
    segment_own, unused_places = token_places(prompt_lengths, token_index)
    window_first = jnp.clip(where_gy - (window_blocks - 1), 0, count_gy - window_blocks)
    source_range = jnp.arange(count_gy, dtype=jnp.int32)[:, None, None]
    block_range = jnp.arange(window_blocks, dtype=jnp.int32)[None, :, None]
    sub_range = jnp.arange(sub, dtype=jnp.int32)[None, None, :]
    key_index = (
        (window_first + block_range) * block_tokens + source_range * sub + sub_range
    ).reshape(window)
    key_segment, unused_places = token_places(prompt_lengths, key_index)
    allowed = (key_segment[None, :] == segment_own[:, None]) & (
        key_index[None, :] <= token_index[:, None]
    )
    score_scale = 1.0 / math.sqrt(HD)
    scores = (
        jnp.einsum("qhd,kd->hqk", queries, key_rows, preferred_element_type=jnp.float32)
        * score_scale
    )
    scores = jnp.where(allowed[None], scores, masked_out)
    row_max = jnp.max(scores, axis=2, keepdims=True)
    weights = jnp.where(allowed[None], jnp.exp(scores - row_max), 0.0)
    totals = jnp.sum(weights, axis=2)
    mixed = jnp.einsum(
        "hqk,kd->hqd", weights.astype(jnp.bfloat16), value_rows, preferred_element_type=jnp.float32
    )
    attention = (
        (mixed / totals[..., None])
        .astype(jnp.bfloat16)
        .transpose(1, 0, 2)
        .reshape(block_tokens, query_cols)
    )
    cache_cols = lax.dynamic_index_in_dim(
        mine_window, where_gy - window_first, 1, keepdims=False
    ).reshape(block_tokens, HD)
    pages_dev = PAGES_DEV
    page_len = block_tokens // pages_dev
    page_range = jnp.arange(pages_dev, dtype=jnp.int32)
    width_cols = cache_cols.shape[1]
    my_pages = cache_cols.reshape(pages_dev, page_len * width_cols)
    capacity = max(1, pages_dev // count_gy)
    slots_all = count_gy * capacity
    owners = (cache_slot // pages_dev).reshape(count_gy, pages_dev)
    earlier = page_range[None, :] < page_range[:, None]
    same_owner = owners[:, :, None] == owners[:, None, :]
    ranks = jnp.sum((same_owner & earlier[None]).astype(jnp.int32), axis=2)
    my_owner = lax.dynamic_index_in_dim(owners, where_gy, 0, keepdims=False)
    my_rank = lax.dynamic_index_in_dim(ranks, where_gy, 0, keepdims=False)
    target = my_owner * capacity + my_rank
    slot_range = jnp.arange(slots_all, dtype=jnp.int32)
    send_map = (slot_range[:, None] == target[None, :]).astype(jnp.bfloat16)
    outgoing = jnp.dot(send_map, my_pages, preferred_element_type=jnp.float32).astype(jnp.bfloat16)
    incoming = lax.all_to_all(outgoing, "gy", split_axis=0, concat_axis=0, tiled=True)
    wanted = where_gy * pages_dev + page_range
    matches = cache_slot[None, :] == wanted[:, None]
    page_ids = jnp.arange(cache_slot.shape[0], dtype=jnp.int32)
    source_page = jnp.sum(jnp.where(matches, page_ids[None, :], 0), axis=1)
    source_rank = jnp.sum(jnp.where(matches, ranks.reshape(-1)[None, :], 0), axis=1)
    source_slot = source_page // pages_dev * capacity + source_rank
    take_map = (source_slot[:, None] == slot_range[None, :]).astype(jnp.bfloat16)
    cache_block = jnp.dot(take_map, incoming, preferred_element_type=jnp.float32)
    cache_block = cache_block.astype(jnp.bfloat16).reshape(pages_dev, page_len, width_cols)
    return (attention, cache_block)


def solution(mesh):
    return jax.shard_map(
        local,
        mesh=mesh,
        in_specs=(P("gx", "gy"), P("gy"), P("gx", "gy"), P(None, "gy"), P(), P()),
        out_specs=(P("gy", "gx"), P("gy", None, "gx")),
        check_vma=False,
    )
```

profile of v0, /device:TPU:2, one launch (start us, length us, event | category | flops | bytes accessed | tf_op | source)
XLA Modules:
  0.0 227.4 jit_solution(1769382629200644866)
XLA Ops:
  8.1 1.7 maximum_maximum_fusion
  9.9 1.0 copy.42
  10.9 23.8 %all_to_all.34 = bf16[4,32,8,128]{3,2,0,1:T(8,128)(2,1)S(1)} all-to-all(bf16[4,32,8,128]{3,2,0,1:T(8,128)(2,1)S(1)} %copy.42), channel_id=1, replica_groups=mesh['gx'=8,'gy'=32] {'gy'}, dimensions={1} | all-to-all | bytes 524288 | tf_op jit(solution)/shard_map/all_to_all | solution.py:65
  34.8 1.8 broadcast_in_dim.67
  36.6 4.7 %all-to-all-start.1 = ((bf16[8,4,32,8,128]{4,3,2,1,0:T(8,128)(2,1)}), bf16[8,4,32,8,128]{4,3,2,1,0:T(8,128)(2,1)S(1)}, u32[]{:S(2)}, u32[]{:S(2)}) async-start(bf16[8,4,32,8,128]{4,3,2,1,0:T(8,128)(2,1)} %broadcast_in_dim.67), calls=%async_computation.1 | async-start | bytes 4194304 | tf_op jit(solution)/shard_map/all_to_all | solution.py:67
  42.3 24.8 %all-to-all-done.1 = bf16[8,4,32,8,128]{4,3,2,1,0:T(8,128)(2,1)S(1)} async-done(((bf16[8,4,32,8,128]{4,3,2,1,0:T(8,128)(2,1)}), bf16[8,4,32,8,128]{4,3,2,1,0:T(8,128)(2,1)S(1)}, u32[]{:S(2)}, u32[]{:S(2)}) %all-to-all-start.1) | async-done | bytes 2097184 | tf_op jit(solution)/shard_map/all_to_all | solution.py:67
  67.7 2.5 %convert_element_type.78 = f32[8,4,32,8,128]{4,3,2,1,0:T(8,128)} convert(bf16[8,4,32,8,128]{4,3,2,1,0:T(8,128)(2,1)S(1)} %all-to-all-done.1) | non-fusion elementwise | flops 1048576 | bytes 6291456 | tf_op jit(solution)/shard_map/convert_element_type | solution.py:69
  70.2 31.7 %all-gather.2.cloned.1.call-done = bf16[648,4096]{1,0:T(8,128)(2,1)} async-done(((bf16[648,128]{1,0:T(8,128)(2,1)}), bf16[648,4096]{1,0:T(8,128)(2,1)}) %all-gather.2.cloned.1.call-update) | async-done | bytes 5308432 | tf_op jit(solution)/shard_map/all_gather | solution.py:60
  102.8 5.6 %fusion.7 = f32[256,640]{1,0:T(8,128)S(1)} fusion(bf16[648,4096]{1,0:T(8,128)(2,1)} %all-gather.2.cloned.1.call-done, f32[256,4096]{1,0:T(8,128)} %bitcast.75, f32[4096]{0:T(1024)S(1)} %bitcast.80, f32[256]{0:T(256)S(1)} %rsqrt.11), kind=kOutput, calls=%fused_computation.10 | convolution fusion | flops 1345323008 | bytes 10109952 | tf_op jit(solution)/shard_map/dot_general | solution.py:77
  110.4 2.5 %gather_fusion = bf16[544,8,128]{2,1,0:T(8,128)(2,1)S(1)} fusion(bf16[32,8,128]{2,1,0:T(8,128)(2,1)S(1)} %fusion.34, s32[1024]{0:T(1024)S(1)} %pad_clamp_fusion), kind=kCustom, calls=%fused_computation | custom fusion | bytes 2230400 | tf_op jit(solution)/shard_map/jit(_take)/gather | solution.py:96
  114.0 1.7 reduce.4
  115.7 1.9 reshape.420
  117.6 9.7 %all-to-all-start.2 = ((bf16[32,2,10752]{2,1,0:T(2,128)(2,1)}), bf16[32,2,10752]{2,1,0:T(2,128)(2,1)}, u32[]{:S(2)}, u32[]{:S(2)}) async-start(bf16[32,2,10752]{2,1,0:T(2,128)(2,1)} %reshape.420), calls=%async_computation.2 | async-start | bytes 2752512 | tf_op jit(solution)/shard_map/all_to_all | solution.py:99
  127.8 4.4 %compare_and_fusion = pred[256,4352]{0,1:T(8,128)(4,1)} fusion(s32[256]{0:T(256)S(1)} %get-tuple-element.29, s32[256]{0:T(256)S(1)} %get-tuple-element.16, s32[4352]{0:T(1024)S(1)} %add.184, s32[4352]{0:T(1024)S(1)} %convert_reduce_fusion), kind=kLoop, calls=%fused_computation.12 | loop fusion | flops 3342336 | bytes 1150976 | tf_op jit(solution)/shard_map/and | solution.py:116
  132.2 25.2 %all-to-all-done.2 = bf16[32,2,10752]{2,1,0:T(2,128)(2,1)} async-done(((bf16[32,2,10752]{2,1,0:T(2,128)(2,1)}), bf16[32,2,10752]{2,1,0:T(2,128)(2,1)}, u32[]{:S(2)}, u32[]{:S(2)}) %all-to-all-start.2) | async-done | bytes 1376288 | tf_op jit(solution)/shard_map/all_to_all | solution.py:99
  157.4 7.8 %reshape.421 = bf16[32,1,21504]{2,1,0:T(2,128)(2,1)S(1)} reshape(bf16[32,2,10752]{2,1,0:T(2,128)(2,1)} %all-to-all-done.2) | data formatting | bytes 2752512
  165.7 1.1 copy-done.1
  169.6 5.4 %all-to-all-start.3 = ((bf16[32,2,1024]{2,1,0:T(2,128)(2,1)}), bf16[32,2,1024]{2,1,0:T(2,128)(2,1)S(1)}, u32[]{:S(2)}, u32[]{:S(2)}) async-start(bf16[32,2,1024]{2,1,0:T(2,128)(2,1)} %reshape.422), calls=%async_computation.3 | async-start | bytes 262144 | tf_op jit(solution)/shard_map/all_to_all | solution.py:157
  175.2 1.0 slice.51
  176.4 9.6 %all-to-all-done.3 = bf16[32,2,1024]{2,1,0:T(2,128)(2,1)S(1)} async-done(((bf16[32,2,1024]{2,1,0:T(2,128)(2,1)}), bf16[32,2,1024]{2,1,0:T(2,128)(2,1)S(1)}, u32[]{:S(2)}, u32[]{:S(2)}) %all-to-all-start.3) | async-done | bytes 131104 | tf_op jit(solution)/shard_map/all_to_all | solution.py:157
  186.9 1.2 broadcast_select_fusion.1
  188.1 8.6 %fusion.22 = f32[4352,256,4]{1,0,2:T(8,128)} fusion(bf16[4352,128,1]{1,0,2:T(8,128)(2,1)S(1)} %bitcast.74, bf16[256,4,128]{2,1,0:T(4,128)(2,1)S(1)} %reshape.401), kind=kOutput, calls=%fused_computation.33 | convolution fusion | flops 1140850688 | bytes 19202048 | tf_op jit(solution)/shard_map/qhd,kd->hqk/dot_general | solution.py:121
  196.7 18.1 %fusion.49 = (f32[4,256]{1,0:T(4,128)S(1)}, bf16[4,256,4352]{1,2,0:T(8,128)(2,1)}) fusion(f32[4352,256,4]{1,0,2:T(8,128)} %fusion.22, pred[256,4352]{0,1:T(8,128)(4,1)S(1)} %copy-done.2), kind=kOutput, calls=%fused_computation.106 | output fusion | flops 35655936 | bytes 27856896 | tf_op jit(solution)/shard_map/sub | solution.py:126
  214.8 5.0 %fusion.18 = bf16[256,4,128]{0,2,1:T(8,128)(2,1)S(1)} fusion(bf16[4352,128,1]{1,0,2:T(8,128)(2,1)S(1)} %bitcast.76, bf16[4,256,4352]{1,2,0:T(8,128)(2,1)} %get-tuple-element.27, f32[256,4]{0,1:T(4,128)S(1)} %bitcast.85), kind=kOutput, calls=%fused_computation.24 | convolution fusion | flops 1141112832 | bytes 10293248 | tf_op jit(solution)/shard_map/hqk,kd->hqd/dot_general | solution.py:128
  (75 shorter events, 12.3 us)
Async XLA Ops:
  7.2 1.0 copy-start
  7.2 94.8 %all-gather.2.cloned.1.call-start = ((), (), s32[]{:S(2)}) async-start(), calls=%async_computation.4 | async-start | bytes 5474304 | tf_op jit(solution)/shard_map/all_gather | solution.py:60
  34.8 6.6 %copy-start.6 = (s32[8]{0:T(128)S(1)}, s32[8]{0:T(128)}, u32[]{:S(2)}) copy-start(s32[8]{0:T(128)} %param.11) | copy-start | bytes 100
  34.8 6.8 %copy-start.5 = (s32[544]{0:T(1024)S(1)}, s32[544]{0:T(1024)}, u32[]{:S(2)}) copy-start(s32[544]{0:T(1024)} %constant.153) | copy-start | bytes 6532
  36.6 30.5 %all-to-all-start.1 = ((bf16[8,4,32,8,128]{4,3,2,1,0:T(8,128)(2,1)}), bf16[8,4,32,8,128]{4,3,2,1,0:T(8,128)(2,1)S(1)}, u32[]{:S(2)}, u32[]{:S(2)}) async-start(bf16[8,4,32,8,128]{4,3,2,1,0:T(8,128)(2,1)} %broadcast_in_dim.67), calls=%async_computation.1 | async-start | bytes 4194304 | tf_op jit(solution)/shard_map/all_to_all | solution.py:67
  117.6 39.8 %all-to-all-start.2 = ((bf16[32,2,10752]{2,1,0:T(2,128)(2,1)}), bf16[32,2,10752]{2,1,0:T(2,128)(2,1)}, u32[]{:S(2)}, u32[]{:S(2)}) async-start(bf16[32,2,10752]{2,1,0:T(2,128)(2,1)} %reshape.420), calls=%async_computation.2 | async-start | bytes 2752512 | tf_op jit(solution)/shard_map/all_to_all | solution.py:99
  165.7 1.1 copy-start.1
  165.7 1.6 copy-start.4
  167.0 19.9 %collective-permute-start = (bf16[32,17,8,128]{3,2,1,0:T(8,128)(2,1)S(1)}, bf16[32,17,8,128]{3,2,1,0:T(8,128)(2,1)S(1)}, u32[]{:S(2)}, u32[]{:S(2)}) collective-permute-start(bf16[32,17,8,128]{3,2,1,0:T(8,128)(2,1)S(1)} %bitcast.71), channel_id=1, source_target_pairs={{0,32},{32,0},{64,96},{96,64},{128,160},{160,128},{192,224},{224,1... | collective-permute-start | bytes 3342344 | tf_op jit(solution)/shard_map/ppermute | solution.py:102
  169.6 16.3 %all-to-all-start.3 = ((bf16[32,2,1024]{2,1,0:T(2,128)(2,1)}), bf16[32,2,1024]{2,1,0:T(2,128)(2,1)S(1)}, u32[]{:S(2)}, u32[]{:S(2)}) async-start(bf16[32,2,1024]{2,1,0:T(2,128)(2,1)} %reshape.422), calls=%async_computation.3 | async-start | bytes 262144 | tf_op jit(solution)/shard_map/all_to_all | solution.py:157
  188.1 8.6 %copy-start.2 = (pred[256,4352]{0,1:T(8,128)(4,1)S(1)}, pred[256,4352]{0,1:T(8,128)(4,1)}, u32[]{:S(2)}) copy-start(pred[256,4352]{0,1:T(8,128)(4,1)} %compare_and_fusion) | copy-start | bytes 3342340
  196.7 18.1 %copy-start.3 = (bf16[32,17,8,128]{3,2,1,0:T(8,128)(2,1)S(1)}, bf16[32,17,8,128]{3,2,1,0:T(8,128)(2,1)}, u32[]{:S(2)}) copy-start(bf16[32,17,8,128]{3,2,1,0:T(8,128)(2,1)} %get-tuple-element.19) | copy-start | bytes 3342340
Sparse Core Ops, SparseCore 0:
  11.0 90.8 all-gather.1
where the time goes:
time: 228 us; the launch traced here: 227 us
  waiting for transfers between devices  91.3 us (40%)
  other arithmetic  35 us (15%)
  blocking collectives  23.8 us (10%)
  local copies, waits for them, and re-layouts  23.2 us (10%)
  starting transfers between devices  20.1 us (9%)
  matrix products  19.5 us (9%)
  between operations  14.4 us (6%)
    all_gather x1, waiting for transfers between devices, local(): gathered = lax.all_gather(stacked, 'gy', axis=1, tiled=True)  31.7 us
    all_to_all x1, waiting for transfers between devices, local(): arrived = lax.all_to_all(parcel, 'gy', 0, 0, tiled=True)  25.2 us
    all_to_all x1, waiting for transfers between devices, local(): rows_here = lax.all_to_all(spread, 'gx', 0, 0, tiled=True)  24.8 us
    all_to_all x1, blocking collectives, local(): pieces = lax.all_to_all(pieces, 'gy', 1, 1, tiled=True)  23.8 us
    sub x1, other arithmetic, local(): weights = jnp.where(allowed[None], jnp.exp(scores - row_max), 0.0)  18.1 us
    unnamed x23, local copies, waits for them, and re-layouts  14.6 us
    all_to_all x1, starting transfers between devices, local(): arrived = lax.all_to_all(parcel, 'gy', 0, 0, tiled=True)  9.68 us
    all_to_all x1, waiting for transfers between devices, local(): lax.all_to_all(outgoing, 'gy', split_axis=0, concat_axis=0, tiled=True)  9.57 us
  transfers between devices with their start and end apart: 5, of which 4 were waited for; matrix products, arithmetic and copies ran while one was open for 7% of the time, Pallas kernels for 0%

commit v1 on v0

--- a/solution.py
+++ b/solution.py
@@ -57,7 +57,9 @@
         [norm_gain[None, :], jnp.zeros((7, local_feats), norm_gain.dtype)], axis=0
     )
     stacked = jnp.concatenate([query_proj, kv_rows, gain_rows], axis=0)
-    gathered = lax.all_gather(stacked, "gy", axis=1, tiled=True)
+    gathered = jnp.concatenate(
+        lax.all_to_all(jnp.stack([stacked] * lax.axis_size("gy")), "gy", 0, 0), axis=1
+    )
     weight_rows = query_cols + HD
     weights_full = gathered[:weight_rows]
     gain_full = gathered[weight_rows]

time: 228 us -> 322 us (1.41)
  waiting for transfers between devices: 91.3 us -> 182 us
  local copies, waits for them, and re-layouts: 23.2 us -> 40.9 us
  between operations: 14.4 us -> 1.06 us
  other arithmetic: 35 us -> 30.8 us
  starting transfers between devices: 20.1 us -> 23.8 us
    all_to_all x0 -> x1, waiting for transfers between devices: none -> 117 us  [local(): lax.all_to_all(jnp.stack([stacked] * lax.axis_size('gy')), 'gy', 0, 0)]
    all_gather x1 -> x0, waiting for transfers between devices: 31.7 us -> none  [local(): gathered = lax.all_gather(stacked, 'gy', axis=1, tiled=True)]
    slice x0 -> x2, local copies, waits for them, and re-layouts: none -> 12.1 us  [local(): weights_full = gathered[:weight_rows]]
    all_to_all x0 -> x1, starting transfers between devices: none -> 5.18 us  [local(): lax.all_to_all(jnp.stack([stacked] * lax.axis_size('gy')), 'gy', 0, 0)]
    all_to_all x1, waiting for transfers between devices: 25.2 us -> 30.4 us  [local(): arrived = lax.all_to_all(parcel, 'gy', 0, 0, tiled=True)]
    all_to_all x0 -> x1, local copies, waits for them, and re-layouts: none -> 3.35 us  [local(): lax.all_to_all(jnp.stack([stacked] * lax.axis_size('gy')), 'gy', 0, 0)]
    unnamed x23 -> x29, local copies, waits for them, and re-layouts: 14.6 us -> 13.8 us
  transfers between devices with their start and end apart: 5 -> 5, of which waited for: 4 -> 4; matrix products, arithmetic and copies ran while one was open for 7% -> 3% of each run, Pallas kernels for 0% -> 0%
where the time goes in v1:
time: 322 us; the launch traced here: 321 us
  waiting for transfers between devices  182 us (57%)
  local copies, waits for them, and re-layouts  40.9 us (13%)
  other arithmetic  30.8 us (10%)
  starting transfers between devices  23.8 us (7%)
  blocking collectives  23.7 us (7%)
  matrix products  18.3 us (6%)
    all_to_all x1, waiting for transfers between devices, local(): lax.all_to_all(jnp.stack([stacked] * lax.axis_size('gy')), 'gy', 0, 0)  117 us
    all_to_all x1, waiting for transfers between devices, local(): arrived = lax.all_to_all(parcel, 'gy', 0, 0, tiled=True)  30.4 us
    all_to_all x1, waiting for transfers between devices, local(): rows_here = lax.all_to_all(spread, 'gx', 0, 0, tiled=True)  25.4 us
    all_to_all x1, blocking collectives, local(): pieces = lax.all_to_all(pieces, 'gy', 1, 1, tiled=True)  23.7 us
    sub x1, other arithmetic, local(): weights = jnp.where(allowed[None], jnp.exp(scores - row_max), 0.0)  18.1 us
    unnamed x29, local copies, waits for them, and re-layouts  13.8 us
    slice x2, local copies, waits for them, and re-layouts, local(): weights_full = gathered[:weight_rows]  12.1 us
    all_to_all x1, waiting for transfers between devices, local(): lax.all_to_all(outgoing, 'gy', split_axis=0, concat_axis=0, tiled=True)  9.57 us
  transfers between devices with their start and end apart: 5, of which 4 were waited for; matrix products, arithmetic and copies ran while one was open for 3% of the time, Pallas kernels for 0%

profile of v1, /device:TPU:2, one launch (start us, length us, event | category | flops | bytes accessed | tf_op | source)
XLA Modules:
  0.0 320.9 jit_solution(5536689947217154078)
XLA Ops:
  1.7 23.7 %all_to_all.39 = bf16[4,32,8,128]{3,2,0,1:T(8,128)(2,1)S(1)} all-to-all(bf16[4,32,8,128]{3,2,0,1:T(8,128)(2,1)S(1)} %copy.55), channel_id=1, replica_groups=mesh['gx'=8,'gy'=32] {'gy'}, dimensions={1} | all-to-all | bytes 524288 | tf_op jit(solution)/shard_map/all_to_all | solution.py:67
  25.5 1.8 broadcast_in_dim.67
  27.3 4.8 %all-to-all-start.1 = ((bf16[8,4,32,8,128]{4,3,2,1,0:T(8,128)(2,1)}), bf16[8,4,32,8,128]{4,3,2,1,0:T(8,128)(2,1)S(1)}, u32[]{:S(2)}, u32[]{:S(2)}) async-start(bf16[8,4,32,8,128]{4,3,2,1,0:T(8,128)(2,1)} %broadcast_in_dim.67), calls=%async_computation.1 | async-start | bytes 4194304 | tf_op jit(solution)/shard_map/all_to_all | solution.py:69
  32.4 25.4 %all-to-all-done.1 = bf16[8,4,32,8,128]{4,3,2,1,0:T(8,128)(2,1)S(1)} async-done(((bf16[8,4,32,8,128]{4,3,2,1,0:T(8,128)(2,1)}), bf16[8,4,32,8,128]{4,3,2,1,0:T(8,128)(2,1)S(1)}, u32[]{:S(2)}, u32[]{:S(2)}) %all-to-all-start.1) | async-done | bytes 2097184 | tf_op jit(solution)/shard_map/all_to_all | solution.py:69
  57.9 3.0 stack.2
  60.9 5.2 %all-to-all-start.2 = ((bf16[32,648,128]{2,1,0:T(8,128)(2,1)}), bf16[32,648,128]{2,1,0:T(8,128)(2,1)}, u32[]{:S(2)}, u32[]{:S(2)}) async-start(bf16[32,648,128]{2,1,0:T(8,128)(2,1)} %stack.2), calls=%async_computation.2 | async-start | bytes 10616832 | tf_op jit(solution)/shard_map/all_to_all | solution.py:61
  67.6 116.9 %all-to-all-done.2 = bf16[32,648,128]{2,1,0:T(8,128)(2,1)} async-done(((bf16[32,648,128]{2,1,0:T(8,128)(2,1)}), bf16[32,648,128]{2,1,0:T(8,128)(2,1)}, u32[]{:S(2)}, u32[]{:S(2)}) %all-to-all-start.2) | async-done | bytes 5308448 | tf_op jit(solution)/shard_map/all_to_all | solution.py:61
  184.5 3.4 %copy.84 = bf16[32,648,128]{2,0,1:T(8,128)(2,1)S(1)} copy(bf16[32,648,128]{2,1,0:T(8,128)(2,1)} %all-to-all-done.2) | data formatting | bytes 10616832 | tf_op jit(solution)/shard_map/all_to_all | solution.py:61
  187.9 3.2 %slice.48 = bf16[640,32,128]{2,1,0:T(8,128)(2,1)} slice(bf16[648,32,128]{2,1,0:T(8,128)(2,1)S(1)} %bitcast.80), slice={[0:640], [0:32], [0:128]} | slice | bytes 10485760 | tf_op jit(solution)/shard_map/slice | solution.py:64
  191.1 8.9 %copy.58 = bf16[640,32,128]{0,2,1:T(8,128)(2,1)} copy(bf16[640,32,128]{2,1,0:T(8,128)(2,1)} %slice.48) | data formatting | bytes 10485760 | tf_op jit(solution)/shard_map/slice | solution.py:64
  200.7 4.3 %fusion.50 = f32[256,640]{1,0:T(8,128)S(1)} fusion(bf16[256,4096]{1,0:T(8,128)(2,1)S(1)} %bitcast.88, bf16[640,4096]{0,1:T(8,128)(2,1)} %bitcast.83), kind=kOutput, calls=%fused_computation.108 | convolution fusion | flops 1342177280 | bytes 7995392 | tf_op jit(solution)/shard_map/dot_general | solution.py:79
  207.0 2.5 gather_fusion
  210.7 1.7 reduce.4
  212.4 1.9 reshape.439
  214.3 8.3 %all-to-all-start.3 = ((bf16[32,2,10752]{2,1,0:T(2,128)(2,1)}), bf16[32,2,10752]{2,1,0:T(2,128)(2,1)}, u32[]{:S(2)}, u32[]{:S(2)}) async-start(bf16[32,2,10752]{2,1,0:T(2,128)(2,1)} %reshape.439), calls=%async_computation.3 | async-start | bytes 2752512 | tf_op jit(solution)/shard_map/all_to_all | solution.py:101
  223.1 4.4 %compare_and_fusion = pred[256,4352]{0,1:T(8,128)(4,1)} fusion(s32[256]{0:T(256)S(1)} %get-tuple-element.31, s32[256]{0:T(256)S(1)} %get-tuple-element.18, s32[4352]{0:T(1024)S(1)} %add.183, s32[4352]{0:T(1024)S(1)} %convert_reduce_fusion), kind=kLoop, calls=%fused_computation.13 | loop fusion | flops 3342336 | bytes 1150976 | tf_op jit(solution)/shard_map/and | solution.py:118
  227.5 30.4 %all-to-all-done.3 = bf16[32,2,10752]{2,1,0:T(2,128)(2,1)} async-done(((bf16[32,2,10752]{2,1,0:T(2,128)(2,1)}), bf16[32,2,10752]{2,1,0:T(2,128)(2,1)}, u32[]{:S(2)}, u32[]{:S(2)}) %all-to-all-start.3) | async-done | bytes 1376288 | tf_op jit(solution)/shard_map/all_to_all | solution.py:101
  257.8 7.8 %reshape.440 = bf16[32,1,21504]{2,1,0:T(2,128)(2,1)S(1)} reshape(bf16[32,2,10752]{2,1,0:T(2,128)(2,1)} %all-to-all-done.3) | data formatting | bytes 2752512
  269.9 5.4 %all-to-all-start.4 = ((bf16[32,2,1024]{2,1,0:T(2,128)(2,1)}), bf16[32,2,1024]{2,1,0:T(2,128)(2,1)S(1)}, u32[]{:S(2)}, u32[]{:S(2)}) async-start(bf16[32,2,1024]{2,1,0:T(2,128)(2,1)} %reshape.441), calls=%async_computation.4 | async-start | bytes 262144 | tf_op jit(solution)/shard_map/all_to_all | solution.py:159
  276.6 9.6 %all-to-all-done.4 = bf16[32,2,1024]{2,1,0:T(2,128)(2,1)S(1)} async-done(((bf16[32,2,1024]{2,1,0:T(2,128)(2,1)}), bf16[32,2,1024]{2,1,0:T(2,128)(2,1)S(1)}, u32[]{:S(2)}, u32[]{:S(2)}) %all-to-all-start.4) | async-done | bytes 131104 | tf_op jit(solution)/shard_map/all_to_all | solution.py:159
  287.1 1.2 broadcast_select_fusion.1
  288.3 8.6 %fusion.21 = f32[4352,256,4]{1,0,2:T(8,128)} fusion(bf16[4352,128,1]{1,0,2:T(8,128)(2,1)S(1)} %bitcast.87, bf16[256,4,128]{2,1,0:T(4,128)(2,1)S(1)} %reshape.421), kind=kOutput, calls=%fused_computation.33 | convolution fusion | flops 1140850688 | bytes 19202048 | tf_op jit(solution)/shard_map/qhd,kd->hqk/dot_general | solution.py:123
  296.9 18.1 %fusion.49 = (f32[4,256]{1,0:T(4,128)S(1)}, bf16[4,256,4352]{1,2,0:T(8,128)(2,1)}) fusion(f32[4352,256,4]{1,0,2:T(8,128)} %fusion.21, pred[256,4352]{0,1:T(8,128)(4,1)S(1)} %copy-done.3), kind=kOutput, calls=%fused_computation.107 | output fusion | flops 35655936 | bytes 27856896 | tf_op jit(solution)/shard_map/sub | solution.py:128
  315.0 5.0 %fusion.17 = bf16[256,4,128]{0,2,1:T(8,128)(2,1)S(1)} fusion(bf16[4352,128,1]{1,0,2:T(8,128)(2,1)S(1)} %bitcast.89, bf16[4,256,4352]{1,2,0:T(8,128)(2,1)} %get-tuple-element.29, f32[256,4]{0,1:T(4,128)S(1)} %bitcast.97), kind=kOutput, calls=%fused_computation.24 | convolution fusion | flops 1141112832 | bytes 10293248 | tf_op jit(solution)/shard_map/hqk,kd->hqd/dot_general | solution.py:130
  (83 shorter events, 14.3 us)
Async XLA Ops:
  0.6 31.6 %copy-start = (bf16[1024,128]{1,0:T(8,128)(2,1)S(1)}, bf16[1024,128]{1,0:T(8,128)(2,1)}, u32[]{:S(2)}) copy-start(bf16[1024,128]{1,0:T(8,128)(2,1)} %param.10) | copy-start | bytes 786436
  25.5 6.8 %copy-start.5 = (bf16[512,128]{1,0:T(8,128)(2,1)S(1)}, bf16[512,128]{1,0:T(8,128)(2,1)}, u32[]{:S(2)}) copy-start(bf16[512,128]{1,0:T(8,128)(2,1)} %param.9) | copy-start | bytes 393220
  25.5 6.8 %copy-start.8 = (bf16[128]{0:T(256)(128)(2,1)S(1)}, bf16[128]{0:T(256)(128)(2,1)}, u32[]{:S(2)}) copy-start(bf16[128]{0:T(256)(128)(2,1)} %param.8) | copy-start | bytes 772
  27.3 30.5 %all-to-all-start.1 = ((bf16[8,4,32,8,128]{4,3,2,1,0:T(8,128)(2,1)}), bf16[8,4,32,8,128]{4,3,2,1,0:T(8,128)(2,1)S(1)}, u32[]{:S(2)}, u32[]{:S(2)}) async-start(bf16[8,4,32,8,128]{4,3,2,1,0:T(8,128)(2,1)} %broadcast_in_dim.67), calls=%async_computation.1 | async-start | bytes 4194304 | tf_op jit(solution)/shard_map/all_to_all | solution.py:69
  60.9 5.2 %copy-start.9 = (s32[8]{0:T(128)S(1)}, s32[8]{0:T(128)}, u32[]{:S(2)}) copy-start(s32[8]{0:T(128)} %param.11) | copy-start | bytes 100
  60.9 5.4 %copy-start.7 = (s32[544]{0:T(1024)S(1)}, s32[544]{0:T(1024)}, u32[]{:S(2)}) copy-start(s32[544]{0:T(1024)} %constant.153) | copy-start | bytes 6532
  60.9 123.6 %all-to-all-start.2 = ((bf16[32,648,128]{2,1,0:T(8,128)(2,1)}), bf16[32,648,128]{2,1,0:T(8,128)(2,1)}, u32[]{:S(2)}, u32[]{:S(2)}) async-start(bf16[32,648,128]{2,1,0:T(8,128)(2,1)} %stack.2), calls=%async_computation.2 | async-start | bytes 10616832 | tf_op jit(solution)/shard_map/all_to_all | solution.py:61
  214.3 43.6 %all-to-all-start.3 = ((bf16[32,2,10752]{2,1,0:T(2,128)(2,1)}), bf16[32,2,10752]{2,1,0:T(2,128)(2,1)}, u32[]{:S(2)}, u32[]{:S(2)}) async-start(bf16[32,2,10752]{2,1,0:T(2,128)(2,1)} %reshape.439), calls=%async_computation.3 | async-start | bytes 2752512 | tf_op jit(solution)/shard_map/all_to_all | solution.py:101
  266.1 1.1 copy-start.2
  266.2 1.4 copy-start.6
  267.5 19.7 %collective-permute-start = (bf16[32,17,8,128]{3,2,1,0:T(8,128)(2,1)S(1)}, bf16[32,17,8,128]{3,2,1,0:T(8,128)(2,1)S(1)}, u32[]{:S(2)}, u32[]{:S(2)}) collective-permute-start(bf16[32,17,8,128]{3,2,1,0:T(8,128)(2,1)S(1)} %bitcast.84), channel_id=1, source_target_pairs={{0,32},{32,0},{64,96},{96,64},{128,160},{160,128},{192,224},{224,1... | collective-permute-start | bytes 3342344 | tf_op jit(solution)/shard_map/ppermute | solution.py:104
  269.9 16.3 %all-to-all-start.4 = ((bf16[32,2,1024]{2,1,0:T(2,128)(2,1)}), bf16[32,2,1024]{2,1,0:T(2,128)(2,1)S(1)}, u32[]{:S(2)}, u32[]{:S(2)}) async-start(bf16[32,2,1024]{2,1,0:T(2,128)(2,1)} %reshape.441), calls=%async_computation.4 | async-start | bytes 262144 | tf_op jit(solution)/shard_map/all_to_all | solution.py:159
  288.3 8.6 %copy-start.3 = (pred[256,4352]{0,1:T(8,128)(4,1)S(1)}, pred[256,4352]{0,1:T(8,128)(4,1)}, u32[]{:S(2)}) copy-start(pred[256,4352]{0,1:T(8,128)(4,1)} %compare_and_fusion) | copy-start | bytes 3342340
  296.9 18.1 %copy-start.4 = (bf16[32,17,8,128]{3,2,1,0:T(8,128)(2,1)S(1)}, bf16[32,17,8,128]{3,2,1,0:T(8,128)(2,1)}, u32[]{:S(2)}) copy-start(bf16[32,17,8,128]{3,2,1,0:T(8,128)(2,1)} %get-tuple-element.21) | copy-start | bytes 3342340
  315.0 5.9 %copy-start.1 = (bf16[1024,128]{1,0:T(8,128)(2,1)S(1)}, bf16[1024,128]{1,0:T(8,128)(2,1)}, u32[]{:S(2)}) copy-start(bf16[1024,128]{1,0:T(8,128)(2,1)} %param.10) | copy-start | bytes 786436
